TPU v7x, 32 devices: a whole 2x2x4 slice. The times are simulated.
32 devices in a mesh: groups: 2 (over y), dp: 4 (over z), tensor: 4 (over x, core).
Axes of the slice: x: 2, y: 2, z: 4, core: 2. Of those that a mesh axis runs over, the one named last changes fastest.
Arguments:
- inputs: bfloat16 [2048, 8192], P(('groups', 'dp'), 'tensor'), parts along dimension 0, may hold values from -6 to 6
- cotangent: bfloat16 [2048, 8192], P(('groups', 'dp'), 'tensor'), parts along dimension 0, may hold values from -6 to 6
- up_blocks: bfloat16 [256, 64, 3, 256], P('dp', 'tensor'), may hold values from -0.21875 to 0.21875
- down_blocks: bfloat16 [256, 64, 3, 256], P('dp', 'tensor'), may hold values from -0.15625 to 0.15625
- low_left: bfloat16 [128, 8192], P(None, 'tensor'), may hold values from -0.0625 to 0.0625
- low_right: bfloat16 [128, 16384], P(None, 'tensor'), may hold values from -0.5 to 0.5
- up_pattern: int32 [64, 3], P('tensor'), may hold values from 0 to 7
- down_pattern: int32 [64, 3], P('tensor'), may hold values from 0 to 7
Outputs:
- grad_input: bfloat16 [2048, 8192], P(('groups', 'dp'), 'tensor'), parts along dimension 0
- grad_up: float32 [512, 64, 3, 256], P(('groups', 'dp'), 'tensor'), parts along dimension 0
- grad_down: float32 [512, 64, 3, 256], P(('groups', 'dp'), 'tensor'), parts along dimension 0
- grad_left: float32 [256, 8192], P(('groups', 'dp'), 'tensor'), parts along dimension 0
- grad_right: float32 [256, 16384], P(('groups', 'dp'), 'tensor'), parts along dimension 0
There are 2 independent parts, one for each index of `groups`. A program takes and returns all parts, laid end to end along the dimension named above; an argument that names none is the same for every part. Nothing has to cross between parts.
Inputs may be any that keep to these rules, and one draw needn't show every extreme that they name: `up_pattern`: feature block within a slice of 8 blocks. `down_pattern`: feature block within a slice of 8 blocks.
All inputs are finite; a program needn't handle non-finite values.
Results may differ from a plain program's by a relative error of at most 0.02.
Values may be sent and summed in bfloat16 or wider, within the bound.
No kernel may reach another device: no remote copies, remote signals or barrier semaphores. Data moves between devices by JAX's collectives and lax.ppermute only.
A program may use at most 128 MiB of HBM per device.

v0:
```python
import math
import jax
import jax.numpy as jnp
from jax import lax
from jax.sharding import PartitionSpec as P

root_coef = 0.7978845608028654
cubic_coef = 0.044715


def swapped(block, axis, distance):
    count = lax.axis_size(axis)
    route = []
    for low in range(count):
        high = low | 1 << distance
        if high != low and high < count:
            route += [(low, high), (high, low)]
    return lax.ppermute(block, axis, route)


def gelu_pair(values):
    inner_arg = root_coef * (values + cubic_coef * values * values * values)
    tangent = jnp.tanh(inner_arg)
    forward = 0.5 * values * (1.0 + tangent)
    slopes = 0.5 * (1.0 + tangent) + 0.5 * values * (1.0 - tangent * tangent) * root_coef * (
        1.0 + 3.0 * cubic_coef * values * values
    )
    return (forward, slopes)


def pick_blocks(slices, pattern, block_size):
    picked = []
    for which_section, source in enumerate(slices):
        shaped = source.reshape(source.shape[0], -1, block_size)
        picked.append(jnp.take(shaped, pattern[:, which_section], axis=1))
    return jnp.stack(picked, axis=2)


def shards(
    inputs, cotangent, up_blocks, down_blocks, low_left, low_right, up_pattern, down_pattern
):
    tokens_here, width_here = inputs.shape
    block_size = up_blocks.shape[3]
    hidden_here = up_blocks.shape[1]
    section_count = up_blocks.shape[2]
    blocks_here = width_here // block_size
    dp_size = lax.axis_size("dp")
    inv_root = 1.0 / math.sqrt(tokens_here * dp_size)
    up_full, down_full = (
        lax.all_gather(up_blocks, "dp", axis=0, tiled=True),
        lax.all_gather(down_blocks, "dp", axis=0, tiled=True),
    )
    sources = [inputs] + [
        swapped(inputs, "tensor", level_bit) for level_bit in range(section_count - 1)
    ]
    selected = pick_blocks(sources, up_pattern, block_size)
    sparse = jnp.einsum("thsi,ihsj->thj", selected, up_full, preferred_element_type=jnp.float32)
    low_part = lax.dot_general(
        inputs, low_left, (((1,), (1,)), ((), ())), preferred_element_type=jnp.float32
    )
    low_sum = lax.psum(low_part.astype(jnp.bfloat16), "tensor")
    preact = sparse.reshape(tokens_here, -1) + jnp.dot(
        low_sum, low_right, preferred_element_type=jnp.float32
    )
    activated, slopes = gelu_pair(preact)
    hidden = activated.astype(jnp.bfloat16)
    picked = pick_blocks([cotangent] * section_count, down_pattern, block_size)
    grad_hidden = jnp.einsum(
        "thso,jhso->thj", picked, down_full, preferred_element_type=jnp.float32
    ).reshape(tokens_here, -1)
    grad_pre = (grad_hidden * slopes).astype(jnp.bfloat16)
    grad_blocks = grad_pre.reshape(tokens_here, hidden_here, block_size)
    slot_ids = jnp.arange(blocks_here, dtype=jnp.int32)

    def section_term(which_section):
        spread = jnp.einsum(
            "thj,ihj->thi",
            grad_blocks,
            up_full[:, :, which_section, :],
            preferred_element_type=jnp.float32,
        )
        placing = (up_pattern[:, which_section][:, None] == slot_ids[None, :]).astype(jnp.float32)
        return jnp.einsum("thi,hd->tdi", spread, placing).reshape(tokens_here, width_here)

    own_term = section_term(0)
    for level_bit in range(section_count - 1):
        outgoing = section_term(level_bit + 1).astype(jnp.bfloat16)
        own_term = own_term + swapped(outgoing, "tensor", level_bit).astype(jnp.float32)
    back_part = lax.dot_general(
        grad_pre, low_right, (((1,), (1,)), ((), ())), preferred_element_type=jnp.float32
    )
    back_low = lax.psum(back_part.astype(jnp.bfloat16), "tensor")
    grad_input = (
        own_term + jnp.dot(back_low, low_left, preferred_element_type=jnp.float32)
    ).astype(jnp.bfloat16)
    row_part = selected
    grad_up = lax.psum_scatter(
        (
            jnp.einsum("thsi,thj->ihsj", row_part, grad_blocks, preferred_element_type=jnp.float32)
            * inv_root
        ).astype(jnp.bfloat16),
        "dp",
        scatter_dimension=0,
        tiled=True,
    ).astype(jnp.float32)
    hidden_blocks = hidden.reshape(tokens_here, hidden_here, block_size)
    row_part = hidden_blocks
    grad_down = lax.psum_scatter(
        (
            jnp.einsum("thj,thso->jhso", row_part, picked, preferred_element_type=jnp.float32)
            * inv_root
        ).astype(jnp.bfloat16),
        "dp",
        scatter_dimension=0,
        tiled=True,
    ).astype(jnp.float32)
    row_part = back_low
    grad_left = lax.psum_scatter(
        (
            lax.dot_general(
                row_part, inputs, (((0,), (0,)), ((), ())), preferred_element_type=jnp.float32
            )
            * inv_root
        ).astype(jnp.bfloat16),
        "dp",
        scatter_dimension=0,
        tiled=True,
    ).astype(jnp.float32)
    row_part = low_sum
    grad_right = lax.psum_scatter(
        (
            lax.dot_general(
                row_part, grad_pre, (((0,), (0,)), ((), ())), preferred_element_type=jnp.float32
            )
            * inv_root
        ).astype(jnp.bfloat16),
        "dp",
        scatter_dimension=0,
        tiled=True,
    ).astype(jnp.float32)
    return (grad_input, grad_up, grad_down, grad_left, grad_right)


def solution(mesh):
    in_specs = (
        P(("groups", "dp"), "tensor"),
        P(("groups", "dp"), "tensor"),
        P("dp", "tensor", None, None),
        P("dp", "tensor", None, None),
        P(None, "tensor"),
        P(None, "tensor"),
        P("tensor", None),
        P("tensor", None),
    )
    out_specs = (
        P(("groups", "dp"), "tensor"),
        P(("groups", "dp"), "tensor", None, None),
        P(("groups", "dp"), "tensor", None, None),
        P(("groups", "dp"), "tensor"),
        P(("groups", "dp"), "tensor"),
    )
    return jax.shard_map(shards, mesh=mesh, in_specs=in_specs, out_specs=out_specs, check_vma=False)
```

profile of v0, /device:TPU:0, one launch (start us, length us, event | category | flops | bytes accessed | tf_op | source)
XLA Modules:
  0.0 590.4 jit_solution(4953019336405703996)
XLA Ops:
  8.1 3.2 copy.60
  11.3 3.2 copy.67
  15.2 3.0 collective-permute-start.1
  32.9 3.4 select_bitcast_fusion.5
  39.3 2.4 select_bitcast_fusion.3
  49.1 4.8 select_bitcast_fusion
  53.9 75.6 %all-gather.3.cloned.1.call-done = bf16[256,16,3,256]{3,0,2,1:T(8,128)(2,1)} async-done(((bf16[64,16,3,256]{3,0,2,1:T(8,128)(2,1)}), bf16[256,16,3,256]{3,0,2,1:T(8,128)(2,1)}) %all-gather.3.cloned.1.call-update) | async-done | bytes 6291472 | tf_op jit(solution)/shard_map/all_gather | solution.py:51
  129.5 7.9 %fusion.17 = f32[16,256,256,1]{1,2,3,0:T(8,128)} fusion(bf16[256,16,3,256]{3,0,2,1:T(8,128)(2,1)} %all-gather.3.cloned.1.call-done, bf16[256,16,1,256]{3,0,2,1:T(8,128)(2,1)S(1)} %copy-done.6, bf16[256,16,1,256]{3,0,2,1:T(8,128)(2,1)} %get-tuple-element.47, bf16[256,16,1,256]{3,0,2,1:T(8,128)(2,1)} %select_bitcast_fusion.5), kind=kOutput, calls=%fused_computation.32 | convolution fusion | flops 1616904192 | bytes 16777216 | tf_op jit(solution)/shard_map/thso,jhso->thj/dot_general | solution.py:68
  137.3 107.2 %all-gather.5.cloned.1.call-done = bf16[256,16,3,256]{3,0,2,1:T(8,128)(2,1)} async-done(((bf16[64,16,3,256]{3,0,2,1:T(8,128)(2,1)}), bf16[256,16,3,256]{3,0,2,1:T(8,128)(2,1)}) %all-gather.5.cloned.1.call-update) | async-done | bytes 6291472 | tf_op jit(solution)/shard_map/all_gather | solution.py:50
  244.6 8.8 %fusion.16 = f32[16,256,256,1]{1,2,3,0:T(8,128)} fusion(bf16[256,16,3,256]{3,0,2,1:T(8,128)(2,1)} %all-gather.5.cloned.1.call-done, bf16[256,16,1,256]{3,0,2,1:T(8,128)(2,1)} %get-tuple-element.48, bf16[256,16,1,256]{3,0,2,1:T(8,128)(2,1)} %get-tuple-element.49, bf16[256,16,1,256]{3,0,2,1:T(8,128)(2,1)} %select_bitcast_fusion.2), kind=kOutput, calls=%fused_computation.31 | convolution fusion | flops 1616904192 | bytes 16777216 | tf_op jit(solution)/shard_map/thsi,ihsj->thj/dot_general | solution.py:57
  253.4 5.7 copy.69
  259.1 5.7 copy.68
  264.8 6.7 %multiply_convert_fusion.2 = (bf16[256,4096]{1,0:T(8,128)(2,1)}, bf16[256,4096]{1,0:T(8,128)(2,1)S(1)}) fusion(f32[256,4096]{1,0:T(8,128)} %copy.69, f32[256,4096]{1,0:T(8,128)} %copy.68, bf16[256,128]{1,0:T(8,128)(2,1)} %all-reduce.3.cloned.1.call-done, bf16[128,4096]{1,0:T(8,128)(2,1)S(1)} %copy-done), kind=kOutput, calls=%fused_computation.30 | convolution fusion | flops 291504128 | bytes 13697024 | tf_op jit(solution)/shard_map/dot_general | solution.py:62
  272.9 29.5 %all-reduce.5.cloned.1.call-done = bf16[256,128]{1,0:T(8,128)(2,1)} async-done(((bf16[256,128]{1,0:T(8,128)(2,1)}), bf16[256,128]{1,0:T(8,128)(2,1)}) %all-reduce.5.cloned.1.call-update) | async-done | bytes 65552 | tf_op jit(solution)/shard_map/psum | solution.py:92
  308.9 6.3 %fusion = bf16[256,16,3,256]{0,3,2,1:T(8,128)(2,1)} fusion(bf16[256,16,1,256]{3,0,2,1:T(8,128)(2,1)S(1)} %copy-done.9, bf16[256,16,1,256]{3,0,2,1:T(8,128)(2,1)S(1)} %copy-done.10, bf16[256,16,1,256]{3,0,2,1:T(8,128)(2,1)} %select_bitcast_fusion.2, bf16[256,16,256,1]{2,1,0,3:T(8,128)(2,1)S(1)} %bitcast.145), kind=kOutput, calls=%fused_computation.8 | convolution fusion | flops 1635778560 | bytes 14680064 | tf_op jit(solution)/shard_map/thsi,thj->ihsj/dot_general | solution.py:99
  315.2 9.1 %copy.77 = bf16[256,16,3,256]{3,1,2,0:T(8,128)(2,1)} copy(bf16[256,16,3,256]{0,3,2,1:T(8,128)(2,1)} %fusion) | data formatting | bytes 12582912 | tf_op jit(solution)/shard_map/convert_element_type | solution.py:101
  324.3 2.4 copy.95
  327.2 6.8 %fusion.1 = bf16[256,16,3,256]{0,3,2,1:T(8,128)(2,1)} fusion(bf16[256,16,1,256]{3,0,2,1:T(8,128)(2,1)S(1)} %copy-done.7, bf16[256,16,1,256]{3,0,2,1:T(8,128)(2,1)S(1)} %copy-done.8, bf16[256,16,1,256]{3,0,2,1:T(8,128)(2,1)} %select_bitcast_fusion.5, bf16[256,16,256,1]{2,1,0,3:T(8,128)(2,1)S(1)} %bitcast.144), kind=kOutput, calls=%fused_computation.9 | convolution fusion | flops 1623195648 | bytes 14680064 | tf_op jit(solution)/shard_map/thj,thso->jhso/dot_general | solution.py:110
  334.0 8.9 %copy.80 = bf16[256,16,3,256]{3,1,2,0:T(8,128)(2,1)} copy(bf16[256,16,3,256]{0,3,2,1:T(8,128)(2,1)} %fusion.1) | data formatting | bytes 12582912 | tf_op jit(solution)/shard_map/convert_element_type | solution.py:112
  355.7 14.6 %collective-permute-done.3 = bf16[256,2048]{1,0:T(8,128)(2,1)S(1)} collective-permute-done((bf16[256,2048]{1,0:T(8,128)(2,1)S(1)}, bf16[256,2048]{1,0:T(8,128)(2,1)S(1)}, u32[]{:S(2)}, u32[]{:S(2)}) %collective-permute-start.3) | collective-permute-done | bytes 1048608 | tf_op jit(solution)/shard_map/ppermute | solution.py:18
  375.3 90.7 %reduce-scatter.5.cloned.1.call-done = bf16[64,16,3,256]{3,1,2,0:T(8,128)(2,1)} async-done(((bf16[256,16,3,256]{3,1,2,0:T(8,128)(2,1)}), bf16[64,16,3,256]{3,1,2,0:T(8,128)(2,1)}) %reduce-scatter.5.cloned.1.call-update) | async-done | bytes 1572880 | tf_op jit(solution)/shard_map/reduce_scatter | solution.py:97
  466.0 3.6 convert_element_type.86
  469.6 109.9 %reduce-scatter.7.cloned.1.call-done = bf16[64,16,3,256]{3,1,2,0:T(8,128)(2,1)} async-done(((bf16[256,16,3,256]{3,1,2,0:T(8,128)(2,1)}), bf16[64,16,3,256]{3,1,2,0:T(8,128)(2,1)}) %reduce-scatter.7.cloned.1.call-update) | async-done | bytes 1572880 | tf_op jit(solution)/shard_map/reduce_scatter | solution.py:108
  579.5 3.5 convert_element_type.90
  (96 shorter events, 51.6 us)
Async XLA Ops:
  8.0 256.8 %copy-start = (bf16[128,4096]{1,0:T(8,128)(2,1)S(1)}, bf16[128,4096]{1,0:T(8,128)(2,1)}, u32[]{:S(2)}) copy-start(bf16[128,4096]{1,0:T(8,128)(2,1)} %param.15) | copy-start | bytes 3145732
  8.0 121.5 %all-gather.3.cloned.1.call-start = ((), (), s32[]{:S(2)}) async-start(), calls=%async_computation.4 | async-start | bytes 7864320 | tf_op jit(solution)/shard_map/all_gather | solution.py:51
  11.3 3.3 copy-start.2
  11.3 233.3 %all-gather.5.cloned.1.call-start = ((), (), s32[]{:S(2)}) async-start(), calls=%async_computation.5 | async-start | bytes 7864320 | tf_op jit(solution)/shard_map/all_gather | solution.py:50
  14.6 250.2 %all-reduce.3.cloned.1.call-start = ((), (), s32[]{:S(2)}) async-start(), calls=%async_computation.6 | async-start | bytes 131072 | tf_op jit(solution)/shard_map/psum | solution.py:61
  15.2 26.8 %collective-permute-start.1 = (bf16[256,2048]{0,1:T(8,128)(2,1)S(1)}, bf16[256,2048]{0,1:T(8,128)(2,1)}, u32[]{:S(2)}, u32[]{:S(2)}) collective-permute-start(bf16[256,2048]{0,1:T(8,128)(2,1)S(1)} %copy.61), channel_id=1, source_target_pairs={{0,2},{2,0},{1,3},{3,1},{4,6},{6,4},{5,7},{7,5},{8,10},{10,8},{9,1... | collective-permute-start | bytes 3145736 | tf_op jit(solution)/shard_map/ppermute | solution.py:18
  18.2 25.3 %collective-permute-start = (bf16[256,2048]{0,1:T(8,128)(2,1)S(1)}, bf16[256,2048]{0,1:T(8,128)(2,1)}, u32[]{:S(2)}, u32[]{:S(2)}) collective-permute-start(bf16[256,2048]{0,1:T(8,128)(2,1)S(1)} %copy.61), channel_id=1, source_target_pairs={{0,1},{1,0},{2,3},{3,2},{4,5},{5,4},{6,7},{7,6},{8,9},{9,8},{10,11... | collective-permute-start | bytes 3145736 | tf_op jit(solution)/shard_map/ppermute | solution.py:18
  20.3 3.9 copy-start.15
  20.3 282.1 %all-reduce.5.cloned.1.call-start = ((), (), s32[]{:S(2)}) async-start(), calls=%async_computation.7 | async-start | bytes 131072 | tf_op jit(solution)/shard_map/psum | solution.py:92
  32.9 3.4 copy-start.5
  36.3 3.0 copy-start.4
  49.1 80.4 %copy-start.6 = (bf16[256,16,1,256]{3,0,2,1:T(8,128)(2,1)S(1)}, bf16[256,16,1,256]{3,0,2,1:T(8,128)(2,1)}, u32[]{:S(2)}) copy-start(bf16[256,16,1,256]{3,0,2,1:T(8,128)(2,1)} %get-tuple-element.46) | copy-start | bytes 6291460
  271.5 33.4 %copy-start.13 = (bf16[256,128]{1,0:T(8,128)(2,1)S(1)}, bf16[256,128]{1,0:T(8,128)(2,1)}, u32[]{:S(2)}) copy-start(bf16[256,128]{1,0:T(8,128)(2,1)} %all-reduce.3.cloned.1.call-done) | copy-start | bytes 196612
  272.8 99.0 %reduce-scatter.9.cloned.1.call-start = ((), (), s32[]{:S(2)}) async-start(), calls=%async_computation.10 | async-start | bytes 655360 | tf_op jit(solution)/shard_map/reduce_scatter | solution.py:118
  304.8 68.7 %reduce-scatter.11.cloned.1.call-start = ((), (), s32[]{:S(2)}) async-start(), calls=%async_computation.11 | async-start | bytes 1310720 | tf_op jit(solution)/shard_map/reduce_scatter | solution.py:130
  306.4 159.6 %reduce-scatter.5.cloned.1.call-start = ((), (), s32[]{:S(2)}) async-start(), calls=%async_computation.8 | async-start | bytes 7864320 | tf_op jit(solution)/shard_map/reduce_scatter | solution.py:97
  324.2 255.2 %reduce-scatter.7.cloned.1.call-start = ((), (), s32[]{:S(2)}) async-start(), calls=%async_computation.9 | async-start | bytes 7864320 | tf_op jit(solution)/shard_map/reduce_scatter | solution.py:108
  324.3 2.4 copy-start.7
  324.3 2.9 copy-start.8
  347.0 23.4 %collective-permute-start.3 = (bf16[256,2048]{1,0:T(8,128)(2,1)S(1)}, bf16[256,2048]{1,0:T(8,128)(2,1)S(1)}, u32[]{:S(2)}, u32[]{:S(2)}) collective-permute-start(bf16[256,2048]{1,0:T(8,128)(2,1)S(1)} %bitcast.146), channel_id=1, source_target_pairs={{0,2},{2,0},{1,3},{3,1},{4,6},{6,4},{5,7},{7,5},{8,10},{10,8},{9,1... | collective-permute-start | bytes 3145736 | tf_op jit(solution)/shard_map/ppermute | solution.py:18
  351.1 19.2 %collective-permute-start.2 = (bf16[256,2048]{1,0:T(8,128)(2,1)S(1)}, bf16[256,2048]{1,0:T(8,128)(2,1)S(1)}, u32[]{:S(2)}, u32[]{:S(2)}) collective-permute-start(bf16[256,2048]{1,0:T(8,128)(2,1)S(1)} %bitcast.147), channel_id=1, source_target_pairs={{0,1},{1,0},{2,3},{3,2},{4,5},{5,4},{6,7},{7,6},{8,9},{9,8},{10,11... | collective-permute-start | bytes 3145736 | tf_op jit(solution)/shard_map/ppermute | solution.py:18
  354.8 15.5 %copy-start.11 = (bf16[128,2048]{1,0:T(8,128)(2,1)S(1)}, bf16[128,2048]{1,0:T(8,128)(2,1)}, u32[]{:S(2)}) copy-start(bf16[128,2048]{1,0:T(8,128)(2,1)} %param.14) | copy-start | bytes 1572868
  354.8 15.5 %copy-start.12 = (bf16[256,128]{1,0:T(8,128)(2,1)S(1)}, bf16[256,128]{1,0:T(8,128)(2,1)}, u32[]{:S(2)}) copy-start(bf16[256,128]{1,0:T(8,128)(2,1)} %all-reduce.5.cloned.1.call-done) | copy-start | bytes 196612
  466.0 117.0 %copy-start.1 = (bf16[128,4096]{1,0:T(8,128)(2,1)S(1)}, bf16[128,4096]{1,0:T(8,128)(2,1)}, u32[]{:S(2)}) copy-start(bf16[128,4096]{1,0:T(8,128)(2,1)} %param.15) | copy-start | bytes 3145732
  (4 other events, 8.2 us)
Sparse Core Ops, SparseCore 0:
  11.4 118.0 all-gather.2
  131.0 113.4 all-gather.4
  305.0 21.8 reduce-scatter.8
  329.0 25.5 reduce-scatter.10
  356.7 109.2 reduce-scatter.4
  468.2 111.2 reduce-scatter.6
Sparse Core Ops, SparseCore 1:
  20.4 31.8 all-reduce.2
  272.9 29.4 all-reduce.4
where the time goes:
time: 592 us; the launch traced here: 590 us
  waiting for transfers between devices  428 us (72%)
  local copies, waits for them, and re-layouts  63.8 us (11%)
  matrix products  56.2 us (9%)
  other arithmetic  22.9 us (4%)
  between operations  15.9 us (3%)
    reduce_scatter x1, waiting for transfers between devices, shards(): lax.psum_scatter((jnp.einsum('thj,thso->jhso', row_part, picked, preferre...  110 us
    all_gather x1, waiting for transfers between devices, shards(): lax.all_gather(up_blocks, 'dp', axis=0, tiled=True)  107 us
    reduce_scatter x1, waiting for transfers between devices, shards(): lax.psum_scatter((jnp.einsum('thsi,thj->ihsj', row_part, grad_blocks, pre...  90.7 us
    all_gather x1, waiting for transfers between devices, shards(): lax.all_gather(down_blocks, 'dp', axis=0, tiled=True)  75.6 us
    psum x1, waiting for transfers between devices, shards(): back_low = lax.psum(back_part.astype(jnp.bfloat16), 'tensor')  29.5 us
    unnamed x41, local copies, waits for them, and re-layouts  17.2 us
    ppermute x4, waiting for transfers between devices, swapped(): return lax.ppermute(block, axis, route)  14.8 us
    another operation x4, other arithmetic, pick_blocks(): return jnp.stack(picked, axis=2)  12.3 us
  transfers between devices with their start and end apart: 12, of which 7 were waited for; matrix products, arithmetic and copies ran while one was open for 21% of the time, Pallas kernels for 0%

commit v1 on v0

--- a/solution.py
+++ b/solution.py
@@ -89,7 +89,7 @@
     back_part = lax.dot_general(
         grad_pre, low_right, (((1,), (1,)), ((), ())), preferred_element_type=jnp.float32
     )
-    back_low = lax.psum(back_part.astype(jnp.bfloat16), "tensor")
+    back_low = jnp.sum(lax.all_gather(back_part.astype(jnp.bfloat16), "tensor"), axis=0)
     grad_input = (
         own_term + jnp.dot(back_low, low_left, preferred_element_type=jnp.float32)
     ).astype(jnp.bfloat16)

time: 592 us -> 566 us (0.956)
  waiting for transfers between devices: 428 us -> 392 us
    psum x1 -> x0, waiting for transfers between devices: 29.5 us -> none  [shards(): back_low = lax.psum(back_part.astype(jnp.bfloat16), 'tensor')]
    unnamed x41 -> x39, local copies, waits for them, and re-layouts: 17.2 us -> 19.2 us
  transfers between devices with their start and end apart: 12 -> 11, of which waited for: 7 -> 6; matrix products, arithmetic and copies ran while one was open for 21% -> 22% of each run, Pallas kernels for 0% -> 0%
where the time goes in v1:
time: 566 us; the launch traced here: 564 us
  waiting for transfers between devices  392 us (69%)
  local copies, waits for them, and re-layouts  65.6 us (12%)
  matrix products  57 us (10%)
  other arithmetic  23 us (4%)
  between operations  15.9 us (3%)
  blocking collectives  5.91 us (1%)
    reduce_scatter x1, waiting for transfers between devices, shards(): lax.psum_scatter((jnp.einsum('thj,thso->jhso', row_part, picked, preferre...  110 us
    all_gather x1, waiting for transfers between devices, shards(): lax.all_gather(up_blocks, 'dp', axis=0, tiled=True)  107 us
    reduce_scatter x1, waiting for transfers between devices, shards(): lax.psum_scatter((jnp.einsum('thsi,thj->ihsj', row_part, grad_blocks, pre...  85.8 us
    all_gather x1, waiting for transfers between devices, shards(): lax.all_gather(down_blocks, 'dp', axis=0, tiled=True)  75.5 us
    unnamed x39, local copies, waits for them, and re-layouts  19.2 us
    ppermute x4, waiting for transfers between devices, swapped(): return lax.ppermute(block, axis, route)  13.3 us
    another operation x4, other arithmetic, pick_blocks(): return jnp.stack(picked, axis=2)  12.3 us
    gather x6, local copies, waits for them, and re-layouts, pick_blocks(): picked.append(jnp.take(shaped, pattern[:, which_section], axis=1))  12.2 us
  transfers between devices with their start and end apart: 11, of which 6 were waited for; matrix products, arithmetic and copies ran while one was open for 22% of the time, Pallas kernels for 0%

profile of v1, /device:TPU:0, one launch (start us, length us, event | category | flops | bytes accessed | tf_op | source)
XLA Modules:
  0.0 564.3 jit_solution(13817751218234281229)
XLA Ops:
  8.1 3.2 copy.60
  11.4 3.2 copy.67
  15.2 3.0 collective-permute-start.1
  33.0 3.4 select_bitcast_fusion.5
  39.4 2.4 select_bitcast_fusion.3
  49.1 4.9 select_bitcast_fusion
  53.9 75.5 %all-gather.4.cloned.1.call-done = bf16[256,16,3,256]{3,0,2,1:T(8,128)(2,1)} async-done(((bf16[64,16,3,256]{3,0,2,1:T(8,128)(2,1)}), bf16[256,16,3,256]{3,0,2,1:T(8,128)(2,1)}) %all-gather.4.cloned.1.call-update) | async-done | bytes 6291472 | tf_op jit(solution)/shard_map/all_gather | solution.py:51
  129.5 7.9 %fusion.17 = f32[16,256,256,1]{1,2,3,0:T(8,128)} fusion(bf16[256,16,3,256]{3,0,2,1:T(8,128)(2,1)} %all-gather.4.cloned.1.call-done, bf16[256,16,1,256]{3,0,2,1:T(8,128)(2,1)S(1)} %copy-done.6, bf16[256,16,1,256]{3,0,2,1:T(8,128)(2,1)} %get-tuple-element.47, bf16[256,16,1,256]{3,0,2,1:T(8,128)(2,1)} %select_bitcast_fusion.5), kind=kOutput, calls=%fused_computation.32 | convolution fusion | flops 1616904192 | bytes 16777216 | tf_op jit(solution)/shard_map/thso,jhso->thj/dot_general | solution.py:68
  137.4 107.3 %all-gather.6.cloned.1.call-done = bf16[256,16,3,256]{3,0,2,1:T(8,128)(2,1)} async-done(((bf16[64,16,3,256]{3,0,2,1:T(8,128)(2,1)}), bf16[256,16,3,256]{3,0,2,1:T(8,128)(2,1)}) %all-gather.6.cloned.1.call-update) | async-done | bytes 6291472 | tf_op jit(solution)/shard_map/all_gather | solution.py:50
  244.6 8.8 %fusion.16 = f32[16,256,256,1]{1,2,3,0:T(8,128)} fusion(bf16[256,16,3,256]{3,0,2,1:T(8,128)(2,1)} %all-gather.6.cloned.1.call-done, bf16[256,16,1,256]{3,0,2,1:T(8,128)(2,1)} %get-tuple-element.48, bf16[256,16,1,256]{3,0,2,1:T(8,128)(2,1)} %get-tuple-element.49, bf16[256,16,1,256]{3,0,2,1:T(8,128)(2,1)} %select_bitcast_fusion.2), kind=kOutput, calls=%fused_computation.31 | convolution fusion | flops 1616904192 | bytes 16777216 | tf_op jit(solution)/shard_map/thsi,ihsj->thj/dot_general | solution.py:57
  253.4 5.7 %copy.69 = f32[256,4096]{1,0:T(8,128)} copy(f32[256,4096]{0,1:T(8,128)} %bitcast.138) | data formatting | bytes 8388608 | tf_op jit(solution)/shard_map/reshape | solution.py:70
  259.1 5.6 %copy.68 = f32[256,4096]{1,0:T(8,128)} copy(f32[256,4096]{0,1:T(8,128)} %bitcast.139) | data formatting | bytes 8388608 | tf_op jit(solution)/shard_map/reshape | solution.py:62
  264.7 6.7 %multiply_convert_fusion.2 = (bf16[256,4096]{1,0:T(8,128)(2,1)}, bf16[256,4096]{1,0:T(8,128)(2,1)S(1)}) fusion(f32[256,4096]{1,0:T(8,128)} %copy.69, f32[256,4096]{1,0:T(8,128)} %copy.68, bf16[256,128]{1,0:T(8,128)(2,1)} %all-reduce.2.cloned.1.call-done, bf16[128,4096]{1,0:T(8,128)(2,1)S(1)} %copy-done), kind=kOutput, calls=%fused_computation.30 | convolution fusion | flops 291504128 | bytes 13697024 | tf_op jit(solution)/shard_map/dot_general | solution.py:62
  272.1 5.9 %all-gather = bf16[1024,128]{1,0:T(8,128)(2,1)S(1)} all-gather(bf16[256,128]{1,0:T(8,128)(2,1)S(1)} %convolution_convert_fusion), channel_id=2, replica_groups=mesh['groups'=2,'dp'=4,'tensor'=4] {'tensor'}, dimensions={0}, use_global_device_ids=true | all-gather | bytes 327680 | tf_op jit(solution)/shard_map/all_gather | solution.py:92
  284.5 6.3 %fusion = bf16[256,16,3,256]{0,3,2,1:T(8,128)(2,1)} fusion(bf16[256,16,1,256]{3,0,2,1:T(8,128)(2,1)S(1)} %copy-done.9, bf16[256,16,1,256]{3,0,2,1:T(8,128)(2,1)S(1)} %copy-done.10, bf16[256,16,1,256]{3,0,2,1:T(8,128)(2,1)} %select_bitcast_fusion.2, bf16[256,16,256,1]{2,1,0,3:T(8,128)(2,1)S(1)} %bitcast.146), kind=kOutput, calls=%fused_computation.8 | convolution fusion | flops 1635778560 | bytes 14680064 | tf_op jit(solution)/shard_map/thsi,thj->ihsj/dot_general | solution.py:99
  290.8 9.0 %copy.77 = bf16[256,16,3,256]{3,1,2,0:T(8,128)(2,1)} copy(bf16[256,16,3,256]{0,3,2,1:T(8,128)(2,1)} %fusion) | data formatting | bytes 12582912 | tf_op jit(solution)/shard_map/convert_element_type | solution.py:101
  302.8 6.8 %fusion.1 = bf16[256,16,3,256]{0,3,2,1:T(8,128)(2,1)} fusion(bf16[256,16,1,256]{3,0,2,1:T(8,128)(2,1)S(1)} %copy-done.7, bf16[256,16,1,256]{3,0,2,1:T(8,128)(2,1)S(1)} %copy-done.8, bf16[256,16,1,256]{3,0,2,1:T(8,128)(2,1)} %select_bitcast_fusion.5, bf16[256,16,256,1]{2,1,0,3:T(8,128)(2,1)S(1)} %bitcast.145), kind=kOutput, calls=%fused_computation.9 | convolution fusion | flops 1623195648 | bytes 14680064 | tf_op jit(solution)/shard_map/thj,thso->jhso/dot_general | solution.py:110
  309.6 8.9 %copy.80 = bf16[256,16,3,256]{3,1,2,0:T(8,128)(2,1)} copy(bf16[256,16,3,256]{0,3,2,1:T(8,128)(2,1)} %fusion.1) | data formatting | bytes 12582912 | tf_op jit(solution)/shard_map/convert_element_type | solution.py:112
  336.2 13.1 %collective-permute-done.3 = bf16[256,2048]{1,0:T(8,128)(2,1)} collective-permute-done((bf16[256,2048]{1,0:T(8,128)(2,1)}, bf16[256,2048]{1,0:T(8,128)(2,1)}, u32[]{:S(2)}, u32[]{:S(2)}) %collective-permute-start.3) | collective-permute-done | bytes 1048608 | tf_op jit(solution)/shard_map/ppermute | solution.py:18
  349.3 3.0 add_convert_fusion
  354.0 85.8 %reduce-scatter.5.cloned.1.call-done = bf16[64,16,3,256]{3,1,2,0:T(8,128)(2,1)} async-done(((bf16[256,16,3,256]{3,1,2,0:T(8,128)(2,1)}), bf16[64,16,3,256]{3,1,2,0:T(8,128)(2,1)}) %reduce-scatter.5.cloned.1.call-update) | async-done | bytes 1572880 | tf_op jit(solution)/shard_map/reduce_scatter | solution.py:97
  439.9 3.6 convert_element_type.88
  443.5 109.9 %reduce-scatter.7.cloned.1.call-done = bf16[64,16,3,256]{3,1,2,0:T(8,128)(2,1)} async-done(((bf16[256,16,3,256]{3,1,2,0:T(8,128)(2,1)}), bf16[64,16,3,256]{3,1,2,0:T(8,128)(2,1)}) %reduce-scatter.7.cloned.1.call-update) | async-done | bytes 1572880 | tf_op jit(solution)/shard_map/reduce_scatter | solution.py:108
  553.3 3.5 convert_element_type.92
  (93 shorter events, 55.0 us)
Async XLA Ops:
  8.0 256.7 %copy-start = (bf16[128,4096]{1,0:T(8,128)(2,1)S(1)}, bf16[128,4096]{1,0:T(8,128)(2,1)}, u32[]{:S(2)}) copy-start(bf16[128,4096]{1,0:T(8,128)(2,1)} %param.15) | copy-start | bytes 3145732
  8.0 121.5 %all-gather.4.cloned.1.call-start = ((), (), s32[]{:S(2)}) async-start(), calls=%async_computation.4 | async-start | bytes 7864320 | tf_op jit(solution)/shard_map/all_gather | solution.py:51
  11.3 3.3 copy-start.2
  11.3 233.3 %all-gather.6.cloned.1.call-start = ((), (), s32[]{:S(2)}) async-start(), calls=%async_computation.5 | async-start | bytes 7864320 | tf_op jit(solution)/shard_map/all_gather | solution.py:50
  14.6 250.1 %all-reduce.2.cloned.1.call-start = ((), (), s32[]{:S(2)}) async-start(), calls=%async_computation.6 | async-start | bytes 131072 | tf_op jit(solution)/shard_map/psum | solution.py:61
  15.2 26.8 %collective-permute-start.1 = (bf16[256,2048]{0,1:T(8,128)(2,1)S(1)}, bf16[256,2048]{0,1:T(8,128)(2,1)}, u32[]{:S(2)}, u32[]{:S(2)}) collective-permute-start(bf16[256,2048]{0,1:T(8,128)(2,1)S(1)} %copy.61), channel_id=1, source_target_pairs={{0,2},{2,0},{1,3},{3,1},{4,6},{6,4},{5,7},{7,5},{8,10},{10,8},{9,1... | collective-permute-start | bytes 3145736 | tf_op jit(solution)/shard_map/ppermute | solution.py:18
  18.2 25.3 %collective-permute-start = (bf16[256,2048]{0,1:T(8,128)(2,1)S(1)}, bf16[256,2048]{0,1:T(8,128)(2,1)}, u32[]{:S(2)}, u32[]{:S(2)}) collective-permute-start(bf16[256,2048]{0,1:T(8,128)(2,1)S(1)} %copy.61), channel_id=1, source_target_pairs={{0,1},{1,0},{2,3},{3,2},{4,5},{5,4},{6,7},{7,6},{8,9},{9,8},{10,11... | collective-permute-start | bytes 3145736 | tf_op jit(solution)/shard_map/ppermute | solution.py:18
  20.3 3.9 copy-start.14
  20.3 314.2 %reduce-scatter.9.cloned.1.call-start = ((), (), s32[]{:S(2)}) async-start(), calls=%async_computation.9 | async-start | bytes 655360 | tf_op jit(solution)/shard_map/reduce_scatter | solution.py:118
  32.9 3.4 copy-start.5
  36.3 2.4 copy-start.3
  36.4 3.0 copy-start.4
  49.1 80.4 %copy-start.6 = (bf16[256,16,1,256]{3,0,2,1:T(8,128)(2,1)S(1)}, bf16[256,16,1,256]{3,0,2,1:T(8,128)(2,1)}, u32[]{:S(2)}) copy-start(bf16[256,16,1,256]{3,0,2,1:T(8,128)(2,1)} %get-tuple-element.46) | copy-start | bytes 6291460
  272.1 8.4 %copy-start.12 = (bf16[256,128]{1,0:T(8,128)(2,1)S(1)}, bf16[256,128]{1,0:T(8,128)(2,1)}, u32[]{:S(2)}) copy-start(bf16[256,128]{1,0:T(8,128)(2,1)} %all-reduce.2.cloned.1.call-done) | copy-start | bytes 196612
  280.5 71.8 %reduce-scatter.11.cloned.1.call-start = ((), (), s32[]{:S(2)}) async-start(), calls=%async_computation.10 | async-start | bytes 1310720 | tf_op jit(solution)/shard_map/reduce_scatter | solution.py:130
  282.1 157.8 %reduce-scatter.5.cloned.1.call-start = ((), (), s32[]{:S(2)}) async-start(), calls=%async_computation.7 | async-start | bytes 7864320 | tf_op jit(solution)/shard_map/reduce_scatter | solution.py:97
  282.3 2.2 copy-start.10
  299.8 253.5 %reduce-scatter.7.cloned.1.call-start = ((), (), s32[]{:S(2)}) async-start(), calls=%async_computation.8 | async-start | bytes 7864320 | tf_op jit(solution)/shard_map/reduce_scatter | solution.py:108
  299.9 2.4 copy-start.7
  299.9 2.9 copy-start.8
  323.5 25.8 %collective-permute-start.3 = (bf16[256,2048]{1,0:T(8,128)(2,1)}, bf16[256,2048]{1,0:T(8,128)(2,1)}, u32[]{:S(2)}, u32[]{:S(2)}) collective-permute-start(bf16[256,2048]{1,0:T(8,128)(2,1)} %bitcast.64), channel_id=1, source_target_pairs={{0,2},{2,0},{1,3},{3,1},{4,6},{6,4},{5,7},{7,5},{8,10},{10,8},{9,1... | collective-permute-start | bytes 3145736 | tf_op jit(solution)/shard_map/ppermute | solution.py:18
  329.9 19.3 %collective-permute-start.2 = (bf16[256,2048]{1,0:T(8,128)(2,1)}, bf16[256,2048]{1,0:T(8,128)(2,1)}, u32[]{:S(2)}, u32[]{:S(2)}) collective-permute-start(bf16[256,2048]{1,0:T(8,128)(2,1)} %bitcast.62), channel_id=1, source_target_pairs={{0,1},{1,0},{2,3},{3,2},{4,5},{5,4},{6,7},{7,6},{8,9},{9,8},{10,11... | collective-permute-start | bytes 3145736 | tf_op jit(solution)/shard_map/ppermute | solution.py:18
  333.6 15.7 %copy-start.11 = (bf16[128,2048]{1,0:T(8,128)(2,1)S(1)}, bf16[128,2048]{1,0:T(8,128)(2,1)}, u32[]{:S(2)}) copy-start(bf16[128,2048]{1,0:T(8,128)(2,1)} %param.14) | copy-start | bytes 1572868
  439.9 117.0 %copy-start.1 = (bf16[128,4096]{1,0:T(8,128)(2,1)S(1)}, bf16[128,4096]{1,0:T(8,128)(2,1)}, u32[]{:S(2)}) copy-start(bf16[128,4096]{1,0:T(8,128)(2,1)} %param.15) | copy-start | bytes 3145732
  (2 other events, 3.7 us)
Sparse Core Ops, SparseCore 0:
  11.4 118.0 all-gather.3
  131.1 113.5 all-gather.5
  280.6 20.0 reduce-scatter.8
  302.8 25.5 reduce-scatter.10
  330.5 109.3 reduce-scatter.4
  442.0 111.2 reduce-scatter.6
Sparse Core Ops, SparseCore 1:
  20.4 31.8 all-reduce.1
